TPU v7x, 512 devices: a whole 4x8x8 slice. The times are simulated.
512 devices in a mesh: req: 64 (over z, x, core), tp: 8 (over y).
Axes of the slice: x: 4, y: 8, z: 8, core: 2. Of those that a mesh axis runs over, the one named last changes fastest.
Arguments:
- queries: bfloat16 [1024, 2048], P('req', 'tp'), may hold values from -27 to 27
- fresh_cache: bfloat16 [1024, 2, 2048], P('req', None, 'tp'), may hold values from -4 to 4
- tail_cache: bfloat16 [1024, 32, 2, 2048], P('req', None, None, 'tp'), may hold values from -4 to 4
- tail_len: int32 [1024], P('req'), may hold values from 1 to 32, as said below
- pool_cache: bfloat16 [2048, 64, 2, 2048], P('req', None, None, 'tp'), may hold values from -4 to 4
- page_group: int32 [2048], P('req'), may hold values from 0 to 63, as said below
- page_start: int32 [2048], P('req'), may hold values from 0 to 16320, as said below
- prompt_len: int32 [64], replicated, may hold values from 1 to 16384, as said below
- residual: bfloat16 [1024, 2048], P('req'), may hold values from -80 to 80
- out_weight: bfloat16 [2048, 2048], P('tp'), may hold values from -0.125 to 0.125
- out_bias: bfloat16 [2048], replicated, may hold values from -0.796875 to 0.796875
- norm_gain: bfloat16 [2048], P('tp'), may hold values from 0.5 to 1.5
- norm_shift: bfloat16 [2048], P('tp'), may hold values from -0.796875 to 0.796875
Outputs:
- attention_out: bfloat16 [1024, 2048], P('req', 'tp')
- normed: bfloat16 [1024, 2048], P('req', 'tp')
Inputs may be any that keep to these rules, and one draw needn't show every extreme that they name: page_group[p] is the group whose prompt page p holds; every page holds some group's prompt; every group holds at least one page and at most 256 pages, and some group holds exactly 256; the pages of a group of n pages lie on min(n, 64) different indices of req, none holding more than ceil(n / 64) of them. The pages of a group of n pages have page_start 0, 64, ..., (n - 1) * 64, each once. `prompt_len`: a group of n pages has a prompt of (n - 1) * 64 + 1 to n * 64 positions. `tail_len`: some request has exactly 32 tail positions.
All inputs are finite; a program needn't handle non-finite values.
Results may differ from a plain program's by a relative error of at most 0.02.
Values may be sent and summed in bfloat16 or wider, within the bound.
No kernel may reach another device: no remote copies, remote signals or barrier semaphores. Data moves between devices by JAX's collectives and lax.ppermute only.
A program may use at most 64 MiB of HBM per device.

v0:
```python
import math
import jax
import jax.numpy as jnp
from jax import lax
from jax.sharding import PartitionSpec as P

HEADS = 16
HEAD = 128
PAGE = 64
masked_score = -1e30
norm_epsilon = 1e-05


def split_halves(values):
    upper_part = lax.optimization_barrier(values.astype(jnp.bfloat16))
    lower_part = (values - upper_part.astype(jnp.float32)).astype(jnp.bfloat16)
    return (upper_part, lower_part)


def local(
    queries,
    fresh_cache,
    tail_cache,
    tail_len,
    pool_cache,
    page_group,
    page_start,
    prompt_len,
    residual,
    out_weight,
    out_bias,
    norm_gain,
    norm_shift,
):
    f32 = jnp.float32
    highest = lax.Precision.HIGHEST
    row_count, feat_width = queries.shape
    heads_here = feat_width // HEAD
    inv_root = 1.0 / math.sqrt(HEAD)
    head_ids = lax.axis_index("tp") * heads_here + jnp.arange(heads_here)
    slopes = jnp.exp2(-8.0 * (head_ids.astype(f32) + 1.0) / HEADS)
    group_count = prompt_len.shape[0]
    page_count = pool_cache.shape[0]
    tail_slots = tail_cache.shape[1]
    n_req = lax.axis_size("req")
    assert group_count == n_req
    everyone = lax.all_gather(queries, "req", axis=0, tiled=True)
    by_group = everyone.reshape(group_count, row_count, heads_here, HEAD)
    safe_group = jnp.clip(page_group, 0, group_count - 1)
    page_queries = by_group[safe_group]
    page_keys = pool_cache[:, :, 0].reshape(page_count, PAGE, heads_here, HEAD)
    page_values = pool_cache[:, :, 1].reshape(page_count, PAGE, heads_here, HEAD)
    prompt_here = prompt_len[safe_group]
    positions = page_start[:, None] + jnp.arange(PAGE)[None, :]
    usable = (positions < prompt_here[:, None]) & (page_group[:, None] >= 0)
    offsets = (positions - prompt_here[:, None]).astype(f32)
    scores = (
        jnp.einsum("pqhd,pshd->pqhs", page_queries, page_keys, preferred_element_type=f32)
        * inv_root
    )
    scores = scores + slopes[None, None, :, None] * offsets[:, None, None, :]
    scores = jnp.where(usable[:, None, None, :], scores, masked_score)
    member = (page_group[:, None] == jnp.arange(group_count)[None, :]) & (page_group[:, None] >= 0)
    page_top = scores.max(-1)
    local_top = jnp.where(member[:, :, None, None], page_top[:, None], masked_score).max(0)
    page_ref = local_top[safe_group]
    weights = jnp.where(usable[:, None, None, :], jnp.exp(scores - page_ref[..., None]), 0.0)
    page_totals = weights.sum(-1)
    upper_part, lower_part = split_halves(weights)
    page_accum = jnp.einsum("pqhs,pshd->pqhd", upper_part, page_values, preferred_element_type=f32)
    page_accum = page_accum + jnp.einsum(
        "pqhs,pshd->pqhd", lower_part, page_values, preferred_element_type=f32
    )
    accum_upper, accum_lower = split_halves(page_accum.reshape(page_count, -1))
    spread = member.T.astype(jnp.bfloat16)
    group_accum = jnp.dot(spread, accum_upper, preferred_element_type=f32)
    group_accum = group_accum + jnp.dot(spread, accum_lower, preferred_element_type=f32)
    group_totals = jnp.dot(
        member.T.astype(f32), page_totals.reshape(page_count, -1), precision=highest
    )
    stats_width = row_count * heads_here
    pad_width = -(group_accum.shape[1] + 2 * stats_width) % 128
    packed = jnp.concatenate(
        [
            group_accum,
            local_top.reshape(group_count, stats_width),
            group_totals,
            jnp.zeros((group_count, pad_width), f32),
        ],
        axis=1,
    )
    arrived = lax.all_to_all(packed, "req", 0, 0, tiled=True)
    accum_width = row_count * feat_width
    part_accum = arrived[:, :accum_width].reshape(n_req, row_count, heads_here, HEAD)
    part_top = arrived[:, accum_width : accum_width + stats_width].reshape(
        n_req, row_count, heads_here
    )
    part_totals = arrived[:, accum_width + stats_width : accum_width + 2 * stats_width].reshape(
        n_req, row_count, heads_here
    )
    home_queries = queries.reshape(row_count, heads_here, HEAD)
    tail_keys = tail_cache[:, :, 0].reshape(row_count, tail_slots, heads_here, HEAD)
    tail_values = tail_cache[:, :, 1].reshape(row_count, tail_slots, heads_here, HEAD)
    fresh_keys = fresh_cache[:, 0].reshape(row_count, heads_here, HEAD)
    fresh_values = fresh_cache[:, 1].reshape(row_count, heads_here, HEAD)
    slot_ids = jnp.arange(tail_slots)
    tail_scores = (
        jnp.einsum("qhd,qjhd->qhj", home_queries, tail_keys, preferred_element_type=f32) * inv_root
    )
    tail_scores = tail_scores + slopes[None, :, None] * slot_ids.astype(f32)[None, None, :]
    tail_scores = jnp.where(
        slot_ids[None, None, :] < tail_len[:, None, None], tail_scores, masked_score
    )
    own_scores = (
        jnp.einsum("qhd,qhd->qh", home_queries, fresh_keys, preferred_element_type=f32) * inv_root
    )
    own_scores = own_scores + slopes[None, :] * tail_len.astype(f32)[:, None]
    home_top = jnp.maximum(tail_scores.max(-1), own_scores)
    row_top = jnp.maximum(home_top, part_top.max(0))
    part_scale = jnp.exp(part_top - row_top[None])
    pool_totals = jnp.sum(part_scale * part_totals, 0)
    pool_accum = jnp.sum(part_scale[..., None] * part_accum, 0)
    tail_weights = jnp.exp(tail_scores - row_top[:, :, None])
    own_weights = jnp.exp(own_scores - row_top)
    totals = tail_weights.sum(-1) + own_weights
    upper_part, lower_part = split_halves(tail_weights)
    accum = jnp.einsum("qhj,qjhd->qhd", upper_part, tail_values, preferred_element_type=f32)
    accum = accum + jnp.einsum("qhj,qjhd->qhd", lower_part, tail_values, preferred_element_type=f32)
    home_accum = accum + own_weights[:, :, None] * fresh_values.astype(f32)
    attention = ((pool_accum + home_accum) / (pool_totals + totals)[:, :, None]).astype(
        jnp.bfloat16
    )
    attention = attention.reshape(row_count, feat_width)
    partial_value = jnp.dot(attention, out_weight, preferred_element_type=f32)
    model_width = residual.shape[1]
    own_start = lax.axis_index("tp") * feat_width
    summed = lax.psum_scatter(
        partial_value.astype(jnp.bfloat16), "tp", scatter_dimension=1, tiled=True
    ).astype(jnp.float32)
    bias_mine = lax.dynamic_slice_in_dim(out_bias, own_start, feat_width, 0).astype(f32)
    attention_mine = (summed + bias_mine[None, :]).astype(jnp.bfloat16)
    residual_mine = lax.dynamic_slice_in_dim(residual, own_start, feat_width, 1).astype(f32)
    hidden_mine = residual_mine + attention_mine.astype(f32)
    first_sum, second_sum = lax.psum(
        (jnp.sum(hidden_mine, -1), jnp.sum(hidden_mine * hidden_mine, -1)), "tp"
    )
    row_mean = (first_sum / model_width)[:, None]
    mean_square = (second_sum / model_width)[:, None]
    row_var = mean_square - row_mean * row_mean
    normed = (
        (hidden_mine - row_mean)
        * lax.rsqrt(row_var + norm_epsilon)
        * norm_gain.astype(f32)[None, :]
    )
    normed = normed + norm_shift.astype(f32)[None, :]
    return (attention_mine, normed.astype(jnp.bfloat16))


def solution(mesh):
    in_specs = (
        P("req", "tp"),
        P("req", None, "tp"),
        P("req", None, None, "tp"),
        P("req"),
        P("req", None, None, "tp"),
        P("req"),
        P("req"),
        P(),
        P("req", None),
        P("tp", None),
        P(),
        P("tp"),
        P("tp"),
    )
    out_specs = (P("req", "tp"), P("req", "tp"))
    return jax.shard_map(local, mesh=mesh, in_specs=in_specs, out_specs=out_specs, check_vma=False)
```

profile of v0, /device:TPU:2, one launch (start us, length us, event | category | flops | bytes accessed | tf_op | source)
XLA Modules:
  0.0 193.3 jit_solution(1942544731091071462)
XLA Ops:
  7.2 0.7 compare_select_fusion
  7.9 0.7 broadcast_compare_fusion
  8.6 1.4 gather_fusion
  10.0 0.7 subtract_convert_fusion.5
  10.7 0.8 fusion.33
  11.5 56.0 %all_gather.3 = bf16[1024,256]{1,0:T(8,128)(2,1)S(1)} all-gather(bf16[16,256]{1,0:T(8,128)(2,1)} %param.13), channel_id=1, replica_groups=mesh['req'=64,'tp'=8] {'req'}, dimensions={0}, use_global_device_ids=true | all-gather | bytes 532480 | tf_op jit(solution)/shard_map/all_gather | solution.py:47
  67.5 0.1 reshape.244
  67.7 0.1 copy.47
  67.7 0.6 gather_fusion.1
  68.3 10.7 %slice_reduce_fusion = (bf16[32,64,256]{2,1,0:T(8,128)(2,1)S(1)}, bf16[32,64,256]{2,1,0:T(8,128)(2,1)S(1)}) fusion(bf16[32,64,2,256]{3,2,1,0:T(2,128)(2,1)} %param.17), kind=kLoop, calls=%fused_computation.7 | loop fusion | bytes 4194304 | tf_op jit(solution)/shard_map/slice | solution.py:52
  79.0 0.1 broadcast_multiply_fusion
  79.1 0.8 fusion.50
  79.9 0.2 select_reduce_fusion
  80.1 0.1 copy.49
  80.2 0.6 gather_fusion.2
  80.8 0.4 fusion.12
  81.2 0.4 fusion.6
  81.6 0.5 fusion.1
  82.1 0.3 copy.52
  82.4 0.4 reshape.245
  82.9 0.4 fusion.48
  83.3 0.4 convolution_add_fusion
  83.7 0.1 copy.54
  83.8 0.3 fusion.42
  84.1 0.1 copy.55
  84.2 0.3 concatenate.3
  84.5 2.1 %copy.57 = f32[64,1,4224]{2,1,0:T(1,128)} copy(f32[64,1,4224]{2,0,1:T(8,128)S(1)} %bitcast.87) | data formatting | bytes 2162688 | tf_op jit(solution)/shard_map/all_to_all | solution.py:92
  86.6 6.3 %all-to-all-start = ((f32[64,1,4224]{2,1,0:T(1,128)}), f32[64,1,4224]{2,1,0:T(1,128)}, u32[]{:S(2)}, u32[]{:S(2)}) async-start(f32[64,1,4224]{2,1,0:T(1,128)} %copy.57), calls=%async_computation | async-start | bytes 2162688 | tf_op jit(solution)/shard_map/all_to_all | solution.py:92
  93.0 0.2 reduce-scatter.2.cloned.1.call-start
  93.3 0.1 fusion.27
  93.4 0.1 copy.72
  93.6 0.1 iota_compare_fusion.1
  93.7 2.2 %slice_reduce_fusion.2 = (bf16[16,32,256]{2,1,0:T(8,128)(2,1)S(1)}, bf16[16,32,256]{2,1,0:T(8,128)(2,1)S(1)}) fusion(bf16[16,32,2,256]{3,2,1,0:T(2,128)(2,1)S(1)} %copy-done.1), kind=kLoop, calls=%fused_computation.22 | loop fusion | bytes 1048576 | tf_op jit(solution)/shard_map/slice | solution.py:103
  95.8 0.2 fusion.18
  96.1 0.1 fusion.44
  96.2 26.2 %all-to-all-done = f32[64,1,4224]{2,1,0:T(1,128)} async-done(((f32[64,1,4224]{2,1,0:T(1,128)}), f32[64,1,4224]{2,1,0:T(1,128)}, u32[]{:S(2)}, u32[]{:S(2)}) %all-to-all-start) | async-done | bytes 1081376 | tf_op jit(solution)/shard_map/all_to_all | solution.py:92
  122.4 3.1 %copy.58 = f32[64,1,4224]{0,2,1:T(8,128)S(1)} copy(f32[64,1,4224]{2,1,0:T(1,128)} %all-to-all-done) | data formatting | bytes 2162688 | tf_op jit(solution)/shard_map/all_to_all | solution.py:92
  125.5 0.1 slice_reduce_fusion.5
  125.6 0.1 reduce_max.42
  125.7 0.1 copy.59
  125.8 0.1 maximum_maximum_fusion
  125.9 0.1 fusion.38
  126.0 0.1 copy.60
  126.0 0.2 fusion.37
  126.2 0.1 sub.80
  126.3 0.7 fusion.26
  127.0 0.7 reduce_sum.62
  127.7 0.6 copy.63
  128.4 1.3 add_add_fusion
  129.7 0.8 copy.61
  130.5 0.8 copy.64
  131.2 0.2 fusion.14
  131.4 0.2 fusion.16
  131.6 0.1 subtract_exponential_fusion.1
  131.7 0.6 fusion
  132.3 0.1 fusion.35
  132.4 0.9 convolution_convert_fusion
  133.3 0.7 convert_element_type.119
  134.0 0.7 convert_element_type.120
  134.7 0.8 dynamic-slice_convert_fusion
  135.4 33.2 %reduce-scatter.2.cloned.1.call-done = bf16[16,256]{1,0:T(8,128)(2,1)} async-done(((bf16[16,2048]{1,0:T(8,128)(2,1)}), bf16[16,256]{1,0:T(8,128)(2,1)}) %reduce-scatter.2.cloned.1.call-update) | async-done | bytes 8208 | tf_op jit(solution)/shard_map/reduce_scatter | solution.py:137
  168.6 0.8 fusion.36
  169.4 15.6 %all-reduce = (f32[16]{0:T(128)S(1)}, f32[16]{0:T(128)S(1)}) all-reduce(f32[16]{0:T(128)S(1)} %get-tuple-element.7, f32[16]{0:T(128)S(1)} %get-tuple-element.6), channel_id=1, replica_groups=mesh['req'=64,'tp'=8] {'tp'}, use_global_device_ids=true, to_apply=%region_12.13 | all-reduce | flops 32 | bytes 256 | tf_op jit(solution)/shard_map/psum | solution.py:144
  185.0 1.4 add_convert_fusion
  (30 shorter events, 0.3 us)
Async XLA Ops:
  7.2 125.3 %copy-start = (bf16[256,2048]{1,0:T(8,128)(2,1)S(1)}, bf16[256,2048]{1,0:T(8,128)(2,1)}, u32[]{:S(2)}) copy-start(bf16[256,2048]{1,0:T(8,128)(2,1)} %param.22) | copy-start | bytes 3145732
  82.1 0.8 copy-start.5
  84.4 8.8 %copy-start.2 = (bf16[16,256]{1,0:T(8,128)(2,1)S(1)}, bf16[16,256]{1,0:T(8,128)(2,1)}, u32[]{:S(2)}) copy-start(bf16[16,256]{1,0:T(8,128)(2,1)} %param.13) | copy-start | bytes 24580
  84.4 8.8 %copy-start.3 = (bf16[16,2,256]{2,1,0:T(2,128)(2,1)S(1)}, bf16[16,2,256]{2,1,0:T(2,128)(2,1)}, u32[]{:S(2)}) copy-start(bf16[16,2,256]{2,1,0:T(2,128)(2,1)} %param.14) | copy-start | bytes 49156
  84.4 9.1 %copy-start.7 = (s32[16]{0:T(128)S(1)}, s32[16]{0:T(128)}, u32[]{:S(2)}) copy-start(s32[16]{0:T(128)} %param.16) | copy-start | bytes 196
  84.5 9.2 %copy-start.1 = (bf16[16,32,2,256]{3,2,1,0:T(2,128)(2,1)S(1)}, bf16[16,32,2,256]{3,2,1,0:T(2,128)(2,1)}, u32[]{:S(2)}) copy-start(bf16[16,32,2,256]{3,2,1,0:T(2,128)(2,1)} %param.15) | copy-start | bytes 1572868
  86.6 35.8 %all-to-all-start = ((f32[64,1,4224]{2,1,0:T(1,128)}), f32[64,1,4224]{2,1,0:T(1,128)}, u32[]{:S(2)}, u32[]{:S(2)}) async-start(f32[64,1,4224]{2,1,0:T(1,128)} %copy.57), calls=%async_computation | async-start | bytes 2162688 | tf_op jit(solution)/shard_map/all_to_all | solution.py:92
  93.0 75.6 %reduce-scatter.2.cloned.1.call-start = ((), (), s32[]{:S(2)}) async-start(), calls=%async_computation.2 | async-start | bytes 73728 | tf_op jit(solution)/shard_map/reduce_scatter | solution.py:137
  93.5 32.3 %copy-start.6 = (f32[16]{0:T(128)}, f32[16]{0:T(128)S(1)}, u32[]{:S(2)}) copy-start(f32[16]{0:T(128)S(1)} %convert_element_type.106) | copy-start | bytes 196
  169.4 17.0 %copy-start.4 = (bf16[16,256]{1,0:T(8,128)(2,1)}, bf16[16,256]{1,0:T(8,128)(2,1)S(1)}, u32[]{:S(2)}) copy-start(bf16[16,256]{1,0:T(8,128)(2,1)S(1)} %get-tuple-element.10) | copy-start | bytes 24580
Sparse Core Ops, SparseCore 0:
  133.5 35.0 reduce-scatter.1
where the time goes:
time: 194 us; the launch traced here: 193 us
  blocking collectives  71.6 us (37%)
  waiting for transfers between devices  59.4 us (31%)
  local copies, waits for them, and re-layouts  25.5 us (13%)
  between operations  14.3 us (7%)
  other arithmetic  11.6 us (6%)
  starting transfers between devices  6.56 us (3%)
  matrix products  4.23 us (2%)
    all_gather x1, blocking collectives, local(): everyone = lax.all_gather(queries, 'req', axis=0, tiled=True)  56 us
    reduce_scatter x1, waiting for transfers between devices, local(): lax.psum_scatter(partial_value.astype(jnp.bfloat16), 'tp', scatter_dimens...  33.2 us
    all_to_all x1, waiting for transfers between devices, local(): arrived = lax.all_to_all(packed, 'req', 0, 0, tiled=True)  26.2 us
    psum x1, blocking collectives, local(): lax.psum((jnp.sum(hidden_mine, -1), jnp.sum(hidden_mine * hidden_mine, -1...  15.6 us
    slice x1, local copies, waits for them, and re-layouts, local(): pool_cache[:, :, 1].reshape(page_count, PAGE, heads_here, HEAD)  10.7 us
    all_to_all x1, starting transfers between devices, local(): arrived = lax.all_to_all(packed, 'req', 0, 0, tiled=True)  6.34 us
    all_to_all x2, local copies, waits for them, and re-layouts, local(): arrived = lax.all_to_all(packed, 'req', 0, 0, tiled=True)  5.25 us
  transfers between devices with their start and end apart: 2, of which 2 were waited for; matrix products, arithmetic and copies ran while one was open for 3% of the time, Pallas kernels for 0%

commit v1 on v0

--- a/solution.py
+++ b/solution.py
@@ -9,6 +9,11 @@
 PAGE = 64
 masked_score = -1e30
 norm_epsilon = 1e-05
+
+
+def gather_by_exchange(x, axis, dim):
+    copies = jnp.concatenate([x] * lax.axis_size(axis), axis=dim)
+    return lax.all_to_all(copies, axis, dim, dim, tiled=True)
 
 
 def split_halves(values):
@@ -44,7 +49,7 @@
     tail_slots = tail_cache.shape[1]
     n_req = lax.axis_size("req")
     assert group_count == n_req
-    everyone = lax.all_gather(queries, "req", axis=0, tiled=True)
+    everyone = gather_by_exchange(queries, "req", 0)
     by_group = everyone.reshape(group_count, row_count, heads_here, HEAD)
     safe_group = jnp.clip(page_group, 0, group_count - 1)
     page_queries = by_group[safe_group]

time: 194 us -> 240 us (1.24)
  local copies, waits for them, and re-layouts: 25.5 us -> 109 us
  blocking collectives: 71.6 us -> 15.6 us
  starting transfers between devices: 6.56 us -> 20.1 us
  waiting for transfers between devices: 59.4 us -> 63.9 us
  other arithmetic: 11.6 us -> 8.9 us
    unnamed x16 -> x83, local copies, waits for them, and re-layouts: 0.04 us -> 81.5 us
    all_gather x1 -> x0, blocking collectives: 56 us -> none  [local(): everyone = lax.all_gather(queries, 'req', axis=0, tiled=True)]
    all_to_all x0 -> x1, starting transfers between devices: none -> 13.9 us  [gather_by_exchange(): return lax.all_to_all(copies, axis, dim, dim, tiled=True)]
    all_to_all x0 -> x1, waiting for transfers between devices: none -> 4.42 us  [gather_by_exchange(): return lax.all_to_all(copies, axis, dim, dim, tiled=True)]
  transfers between devices with their start and end apart: 2 -> 3, of which waited for: 2 -> 3; matrix products, arithmetic and copies ran while one was open for 3% -> 8% of each run, Pallas kernels for 0% -> 0%
where the time goes in v1:
time: 240 us; the launch traced here: 237 us
  local copies, waits for them, and re-layouts  109 us (45%)
  waiting for transfers between devices  63.9 us (27%)
  starting transfers between devices  20.1 us (8%)
  blocking collectives  15.6 us (6%)
  between operations  14.4 us (6%)
  other arithmetic  8.9 us (4%)
  matrix products  5.45 us (2%)
    unnamed x83, local copies, waits for them, and re-layouts  81.5 us
    reduce_scatter x1, waiting for transfers between devices, local(): lax.psum_scatter(partial_value.astype(jnp.bfloat16), 'tp', scatter_dimens...  33.2 us
    all_to_all x1, waiting for transfers between devices, local(): arrived = lax.all_to_all(packed, 'req', 0, 0, tiled=True)  26.2 us
    psum x1, blocking collectives, local(): lax.psum((jnp.sum(hidden_mine, -1), jnp.sum(hidden_mine * hidden_mine, -1...  15.6 us
    all_to_all x1, starting transfers between devices, gather_by_exchange(): return lax.all_to_all(copies, axis, dim, dim, tiled=True)  13.9 us
    slice x1, local copies, waits for them, and re-layouts, local(): pool_cache[:, :, 1].reshape(page_count, PAGE, heads_here, HEAD)  12.1 us
    all_to_all x1, starting transfers between devices, local(): arrived = lax.all_to_all(packed, 'req', 0, 0, tiled=True)  6.05 us
    all_to_all x2, local copies, waits for them, and re-layouts, local(): arrived = lax.all_to_all(packed, 'req', 0, 0, tiled=True)  5.25 us
  transfers between devices with their start and end apart: 3, of which 3 were waited for; matrix products, arithmetic and copies ran while one was open for 8% of the time, Pallas kernels for 0%

profile of v1, /device:TPU:2, one launch (start us, length us, event | category | flops | bytes accessed | tf_op | source)
XLA Modules:
  0.0 237.2 jit_solution(11250782179162156290)
XLA Ops:
  7.2 1.4 constant_dynamic-update-slice_fusion.63
  8.6 1.3 constant_dynamic-update-slice_fusion.62
  9.9 1.3 constant_dynamic-update-slice_fusion.61
  12.5 1.3 constant_dynamic-update-slice_fusion.59
  13.7 1.3 constant_dynamic-update-slice_fusion.58
  15.0 1.3 constant_dynamic-update-slice_fusion.57
  16.3 1.3 constant_dynamic-update-slice_fusion.56
  17.6 1.3 constant_dynamic-update-slice_fusion.55
  18.9 1.3 constant_dynamic-update-slice_fusion.54
  20.2 1.3 constant_dynamic-update-slice_fusion.53
  24.1 1.3 constant_dynamic-update-slice_fusion.50
  25.4 1.3 constant_dynamic-update-slice_fusion.49
  26.7 1.3 constant_dynamic-update-slice_fusion.48
  29.3 1.3 constant_dynamic-update-slice_fusion.46
  30.5 1.3 constant_dynamic-update-slice_fusion.45
  31.8 1.3 constant_dynamic-update-slice_fusion.44
  33.1 1.3 constant_dynamic-update-slice_fusion.43
  34.4 1.3 constant_dynamic-update-slice_fusion.42
  35.7 1.3 constant_dynamic-update-slice_fusion.41
  37.0 1.3 constant_dynamic-update-slice_fusion.40
  38.3 1.3 constant_dynamic-update-slice_fusion.39
  39.6 1.3 constant_dynamic-update-slice_fusion.38
  42.2 1.3 constant_dynamic-update-slice_fusion.36
  43.5 1.3 constant_dynamic-update-slice_fusion.35
  44.7 1.3 constant_dynamic-update-slice_fusion.34
  46.0 1.3 constant_dynamic-update-slice_fusion.33
  47.3 1.3 constant_dynamic-update-slice_fusion.32
  48.6 1.3 constant_dynamic-update-slice_fusion.31
  51.2 1.3 constant_dynamic-update-slice_fusion.29
  52.5 1.3 constant_dynamic-update-slice_fusion.28
  55.1 1.3 constant_dynamic-update-slice_fusion.26
  56.4 1.3 constant_dynamic-update-slice_fusion.25
  57.7 1.3 constant_dynamic-update-slice_fusion.24
  60.2 1.3 constant_dynamic-update-slice_fusion.22
  61.5 1.3 constant_dynamic-update-slice_fusion.21
  64.1 1.3 constant_dynamic-update-slice_fusion.19
  65.4 1.3 constant_dynamic-update-slice_fusion.18
  68.0 1.3 constant_dynamic-update-slice_fusion.16
  70.6 1.3 constant_dynamic-update-slice_fusion.14
  71.9 1.3 constant_dynamic-update-slice_fusion.13
  73.1 1.3 constant_dynamic-update-slice_fusion.12
  74.4 1.3 constant_dynamic-update-slice_fusion.11
  75.7 1.3 constant_dynamic-update-slice_fusion.10
  78.3 1.3 constant_dynamic-update-slice_fusion.8
  79.6 1.3 constant_dynamic-update-slice_fusion.7
  80.9 1.3 constant_dynamic-update-slice_fusion.6
  83.5 1.3 constant_dynamic-update-slice_fusion.4
  84.8 1.3 constant_dynamic-update-slice_fusion.3
  86.1 1.3 constant_dynamic-update-slice_fusion.2
  87.4 1.3 constant_dynamic-update-slice_fusion.1
  88.6 1.3 constant_dynamic-update-slice_fusion
  89.9 13.9 %all-to-all-start = ((bf16[64,16,256]{2,1,0:T(8,128)(2,1)}), bf16[64,16,256]{2,1,0:T(8,128)(2,1)S(1)}, u32[]{:S(2)}, u32[]{:S(2)}) async-start(bf16[64,16,256]{2,1,0:T(8,128)(2,1)} %bitcast), calls=%async_computation | async-start | bytes 1048576 | tf_op jit(solution)/shard_map/all_to_all | solution.py:16
  104.9 12.1 %slice_reduce_fusion = (bf16[32,64,256]{2,1,0:T(8,128)(2,1)S(1)}, bf16[32,64,256]{2,1,0:T(8,128)(2,1)}) fusion(bf16[32,64,2,256]{3,2,1,0:T(2,128)(2,1)} %param.17), kind=kLoop, calls=%fused_computation.7 | loop fusion | bytes 4194304 | tf_op jit(solution)/shard_map/slice | solution.py:57
  116.9 4.4 %all-to-all-done = bf16[64,16,256]{2,1,0:T(8,128)(2,1)S(1)} async-done(((bf16[64,16,256]{2,1,0:T(8,128)(2,1)}), bf16[64,16,256]{2,1,0:T(8,128)(2,1)S(1)}, u32[]{:S(2)}, u32[]{:S(2)}) %all-to-all-start) | async-done | bytes 524320 | tf_op jit(solution)/shard_map/all_to_all | solution.py:16
  122.1 2.0 fusion.50
  128.6 2.1 copy.57
  130.8 6.0 %all-to-all-start.1 = ((f32[64,1,4224]{2,1,0:T(1,128)}), f32[64,1,4224]{2,1,0:T(1,128)}, u32[]{:S(2)}, u32[]{:S(2)}) async-start(f32[64,1,4224]{2,1,0:T(1,128)} %copy.57), calls=%async_computation.1 | async-start | bytes 2162688 | tf_op jit(solution)/shard_map/all_to_all | solution.py:97
  137.5 2.2 slice_reduce_fusion.2
  140.0 26.2 %all-to-all-done.1 = f32[64,1,4224]{2,1,0:T(1,128)} async-done(((f32[64,1,4224]{2,1,0:T(1,128)}), f32[64,1,4224]{2,1,0:T(1,128)}, u32[]{:S(2)}, u32[]{:S(2)}) %all-to-all-start.1) | async-done | bytes 1081376 | tf_op jit(solution)/shard_map/all_to_all | solution.py:97
  166.3 3.1 %copy.58 = f32[64,1,4224]{0,2,1:T(8,128)S(1)} copy(f32[64,1,4224]{2,1,0:T(1,128)} %all-to-all-done.1) | data formatting | bytes 2162688 | tf_op jit(solution)/shard_map/all_to_all | solution.py:97
  172.3 1.3 add_add_fusion
  179.3 33.2 %reduce-scatter.2.cloned.1.call-done = bf16[16,256]{1,0:T(8,128)(2,1)} async-done(((bf16[16,2048]{1,0:T(8,128)(2,1)}), bf16[16,256]{1,0:T(8,128)(2,1)}) %reduce-scatter.2.cloned.1.call-update) | async-done | bytes 8208 | tf_op jit(solution)/shard_map/reduce_scatter | solution.py:142
  213.4 15.6 %all-reduce = (f32[16]{0:T(128)S(1)}, f32[16]{0:T(128)S(1)}) all-reduce(f32[16]{0:T(128)S(1)} %get-tuple-element.7, f32[16]{0:T(128)S(1)} %get-tuple-element.6), channel_id=1, replica_groups=mesh['req'=64,'tp'=8] {'tp'}, use_global_device_ids=true, to_apply=%region_12.13 | all-reduce | flops 32 | bytes 256 | tf_op jit(solution)/shard_map/psum | solution.py:149
  229.0 1.4 add_convert_fusion
  (98 shorter events, 33.2 us)
Async XLA Ops:
  7.2 169.2 %copy-start = (bf16[256,2048]{1,0:T(8,128)(2,1)S(1)}, bf16[256,2048]{1,0:T(8,128)(2,1)}, u32[]{:S(2)}) copy-start(bf16[256,2048]{1,0:T(8,128)(2,1)} %param.22) | copy-start | bytes 3145732
  7.2 96.6 %copy-start.6 = (s32[32]{0:T(128)S(1)}, s32[32]{0:T(128)}, u32[]{:S(2)}) copy-start(s32[32]{0:T(128)} %param.18) | copy-start | bytes 388
  7.2 96.7 %copy-start.1 = (s32[64]{0:T(128)S(1)}, s32[64]{0:T(128)}, u32[]{:S(2)}) copy-start(s32[64]{0:T(128)} %param.20) | copy-start | bytes 772
  7.2 97.4 %copy-start.8 = (s32[32]{0:T(128)S(1)}, s32[32]{0:T(128)}, u32[]{:S(2)}) copy-start(s32[32]{0:T(128)} %param.19) | copy-start | bytes 388
  89.9 31.4 %all-to-all-start = ((bf16[64,16,256]{2,1,0:T(8,128)(2,1)}), bf16[64,16,256]{2,1,0:T(8,128)(2,1)S(1)}, u32[]{:S(2)}, u32[]{:S(2)}) async-start(bf16[64,16,256]{2,1,0:T(8,128)(2,1)} %bitcast), calls=%async_computation | async-start | bytes 1048576 | tf_op jit(solution)/shard_map/all_to_all | solution.py:16
  128.6 8.5 %copy-start.2 = (bf16[16,256]{1,0:T(8,128)(2,1)S(1)}, bf16[16,256]{1,0:T(8,128)(2,1)}, u32[]{:S(2)}) copy-start(bf16[16,256]{1,0:T(8,128)(2,1)} %param.13) | copy-start | bytes 24580
  128.6 8.5 %copy-start.4 = (bf16[16,2,256]{2,1,0:T(2,128)(2,1)S(1)}, bf16[16,2,256]{2,1,0:T(2,128)(2,1)}, u32[]{:S(2)}) copy-start(bf16[16,2,256]{2,1,0:T(2,128)(2,1)} %param.14) | copy-start | bytes 49156
  128.6 8.8 %copy-start.9 = (s32[16]{0:T(128)S(1)}, s32[16]{0:T(128)}, u32[]{:S(2)}) copy-start(s32[16]{0:T(128)} %param.16) | copy-start | bytes 196
  128.6 8.9 %copy-start.3 = (bf16[16,32,2,256]{3,2,1,0:T(2,128)(2,1)S(1)}, bf16[16,32,2,256]{3,2,1,0:T(2,128)(2,1)}, u32[]{:S(2)}) copy-start(bf16[16,32,2,256]{3,2,1,0:T(2,128)(2,1)} %param.15) | copy-start | bytes 1572868
  130.8 35.5 %all-to-all-start.1 = ((f32[64,1,4224]{2,1,0:T(1,128)}), f32[64,1,4224]{2,1,0:T(1,128)}, u32[]{:S(2)}, u32[]{:S(2)}) async-start(f32[64,1,4224]{2,1,0:T(1,128)} %copy.57), calls=%async_computation.1 | async-start | bytes 2162688 | tf_op jit(solution)/shard_map/all_to_all | solution.py:97
  136.8 75.7 %reduce-scatter.2.cloned.1.call-start = ((), (), s32[]{:S(2)}) async-start(), calls=%async_computation.3 | async-start | bytes 73728 | tf_op jit(solution)/shard_map/reduce_scatter | solution.py:142
  137.4 32.3 %copy-start.7 = (f32[16]{0:T(128)}, f32[16]{0:T(128)S(1)}, u32[]{:S(2)}) copy-start(f32[16]{0:T(128)S(1)} %convert_element_type.106) | copy-start | bytes 196
  213.4 17.0 %copy-start.5 = (bf16[16,256]{1,0:T(8,128)(2,1)}, bf16[16,256]{1,0:T(8,128)(2,1)S(1)}, u32[]{:S(2)}) copy-start(bf16[16,256]{1,0:T(8,128)(2,1)S(1)} %get-tuple-element.10) | copy-start | bytes 24580
Sparse Core Ops, SparseCore 0:
  177.3 35.1 reduce-scatter.1
